TPU v7x, 256 devices: a whole 4x4x8 slice. The times are simulated.
256 devices in a mesh: req: 16 (over x, y), cuts: 16 (over z, core).
Axes of the slice: x: 4, y: 4, z: 8, core: 2. Of those that a mesh axis runs over, the one named last changes fastest.
Arguments:
- queries: bfloat16 [16, 2048, 1024], P('req', 'cuts')
- new_keys: bfloat16 [16, 2048, 1024], P('req', 'cuts'), may hold values from -6 to 6
- new_values: bfloat16 [16, 2048, 1024], P('req', 'cuts'), may hold values from -12 to 12
- cache_keys: bfloat16 [16, 4096, 1024], P('req', 'cuts')
- cache_values: bfloat16 [16, 4096, 1024], P('req', 'cuts'), may hold values from -12 to 12
- cache_lengths: int32 [16], P('req'), may hold values from 2 to 4096, as said below
- relative_bias: float32 [16, 32], replicated, may hold values from -4 to 4
- residual: bfloat16 [16, 2048, 1024], P('req', 'cuts')
- out_weight: bfloat16 [1024, 1024], replicated, may hold values from -0.1875 to 0.1875
- norm_gain: bfloat16 [1024], replicated, may hold values from 0.5 to 1.5
- router_weight: bfloat16 [1024, 16], replicated, may hold values from -0.1875 to 0.1875
- routes: int32 [16, 2048, 2], P('req', 'cuts'), may hold values from 0 to 15, all different within a row; in each aligned block of 128 rows (0 to 127, 128 to 255, ..., all dimensions but the last counted through in order) at most 20 rows name the same one
- gate_weight: bfloat16 [16, 1024, 2816], P('req', None, 'cuts'), may hold values from -0.1875 to 0.1875
- up_weight: bfloat16 [16, 1024, 2816], P('req', None, 'cuts'), may hold values from -0.1875 to 0.1875
- down_weight: bfloat16 [16, 1024, 2816], P('req', None, 'cuts'), may hold values from -0.109375 to 0.109375
Outputs:
- layer_out: bfloat16 [16, 2048, 1024], P('req', 'cuts')
Inputs may be any that keep to these rules, and one draw needn't show every extreme that they name: `cache_lengths`: each cached length lies under 256 or above 3840; some request's cache is full. `routes`: among the 128 tokens of one device no expert is named by more than 20 tokens, a bound that some block reaches.
All inputs are finite; a program needn't handle non-finite values.
Results may differ from a plain program's by a relative error of at most 0.03.
Values may be sent and summed in bfloat16 or wider, within the bound.
No kernel may reach another device: no remote copies, remote signals or barrier semaphores. Data moves between devices by JAX's collectives and lax.ppermute only.
A program may use at most 128 MiB of HBM per device.

v0:
```python
from functools import partial
import jax
import jax.numpy as jnp
import numpy as np
from jax import lax
from jax.sharding import PartitionSpec as P

MAXDIST = 128


def shortened(value):
    return jax.tree.map(lambda a: a.astype(jnp.bfloat16) if a.dtype == jnp.float32 else a, value)


def bucket_number(distance, bucket_count, reach_limit):
    exact_count = bucket_count // 2
    if distance < exact_count:
        return distance
    level_value = exact_count + int(
        np.floor(exact_count * np.log(distance / exact_count) / np.log(reach_limit / exact_count))
    )
    return min(bucket_count - 1, level_value)


def bucket_edges(bucket_count, reach_limit):
    edge_list = []
    for target in range(1, bucket_count):
        probe_value = 0
        while bucket_number(probe_value, bucket_count, reach_limit) < target:
            probe_value += 1
        edge_list.append(probe_value)
    return edge_list


def bucket_index(distance, edge_list):
    bucket_level = jnp.zeros(distance.shape, jnp.int32)
    for edge_value in edge_list:
        bucket_level = bucket_level + (distance >= edge_value).astype(jnp.int32)
    return bucket_level


def block_masks(block_index, length, cache_rows, q_rows, query_total, bucket_count):
    cache_slots = block_index * cache_rows + jnp.arange(cache_rows, dtype=jnp.int32)
    new_slots = block_index * q_rows + jnp.arange(q_rows, dtype=jnp.int32)
    key_pos = jnp.concatenate([cache_slots, length + new_slots])
    key_live = jnp.concatenate([cache_slots < length, new_slots >= 0])
    query_pos = length + jnp.arange(query_total, dtype=jnp.int32)
    visible = key_live[None, :] & (key_pos[None, :] <= query_pos[:, None])
    distance = jnp.maximum(query_pos[:, None] - key_pos[None, :], 0)
    return (visible, bucket_index(distance, bucket_edges(bucket_count, MAXDIST)))


def head_partial(visible, bucket, operands):
    query_rows, key_rows, value_rows, bias_table = operands
    scores = (
        lax.dot_general(
            query_rows, key_rows, (((1,), (1,)), ((), ())), preferred_element_type=jnp.float32
        )
        / 8.0
    )
    masked = jnp.where(visible, scores + jnp.take(bias_table, bucket), -1e30)
    block_peak = jnp.max(masked, axis=1)
    weights = jnp.where(visible, jnp.exp(masked - block_peak[:, None]), 0.0)
    block_total = jnp.sum(weights, axis=1)
    numerator = jnp.dot(
        weights.astype(jnp.bfloat16), value_rows, preferred_element_type=jnp.float32
    )
    block_out = (numerator / jnp.maximum(block_total, 1.0)[:, None]).astype(jnp.bfloat16)
    return (block_out, block_peak, block_total)


def block_partials(query_rows, key_rows, value_rows, tables, visible, bucket):
    head_count = tables.shape[0]
    head_dim = query_rows.shape[1] // head_count
    head_queries = query_rows.reshape(query_rows.shape[0], head_count, head_dim).transpose(1, 0, 2)
    head_keys = key_rows.reshape(key_rows.shape[0], head_count, head_dim).transpose(1, 0, 2)
    head_values = value_rows.reshape(value_rows.shape[0], head_count, head_dim).transpose(1, 0, 2)
    return lax.map(
        partial(head_partial, visible, bucket), (head_queries, head_keys, head_values, tables)
    )


def merge_blocks(block_out, block_peak, block_total):
    best_peak = jnp.max(block_peak, axis=0)
    factor = jnp.exp(block_peak - best_peak[None]) * block_total
    weighted = jnp.sum(factor[..., None] * block_out.astype(jnp.float32), axis=0)
    return (weighted / jnp.sum(factor, axis=0)[..., None]).astype(jnp.bfloat16)


def expert_part(row_block, gate_piece, up_piece, down_piece):
    gate_act = jnp.einsum(
        "necd,edf->necf", row_block, gate_piece, preferred_element_type=jnp.float32
    )
    up_act = jnp.einsum("necd,edf->necf", row_block, up_piece, preferred_element_type=jnp.float32)
    act_rows = (jax.nn.gelu(gate_act) * up_act).astype(jnp.bfloat16)
    return jnp.einsum("necf,edf->necd", act_rows, down_piece, preferred_element_type=jnp.float32)


def per_device(
    queries,
    new_keys,
    new_values,
    cache_keys,
    cache_values,
    cache_lengths,
    relative_bias,
    residual,
    out_weight,
    norm_gain,
    router_weight,
    routes,
    gate_weight,
    up_weight,
    down_weight,
):
    cut_count = lax.axis_size("cuts")
    cut_index = lax.axis_index("cuts")
    q_rows = queries.shape[1]
    cache_rows = cache_keys.shape[1]
    model_width = queries.shape[2]
    head_count = relative_bias.shape[0]
    head_dim = model_width // head_count
    bucket_count = relative_bias.shape[1]
    length = cache_lengths[0]
    query_total = q_rows * cut_count
    local_keys = jnp.concatenate([cache_keys[0], new_keys[0]], axis=0)
    local_values = jnp.concatenate([cache_values[0], new_values[0]], axis=0)
    every_query = lax.all_gather(queries[0], "cuts", axis=0, tiled=True)
    visible, bucket = block_masks(cut_index, length, cache_rows, q_rows, query_total, bucket_count)
    block_out, block_peak, block_total = block_partials(
        every_query, local_keys, local_values, relative_bias, visible, bucket
    )
    block_out = block_out.transpose(1, 0, 2).reshape(cut_count, q_rows, model_width)
    block_peak = block_peak.T.reshape(cut_count, q_rows, head_count)
    block_total = block_total.T.reshape(cut_count, q_rows, head_count)
    block_out = lax.all_to_all(
        shortened(block_out), "cuts", split_axis=0, concat_axis=0, tiled=True
    ).astype(block_out.dtype)
    block_peak, block_total = (
        lax.all_to_all(
            shortened(block_peak), "cuts", split_axis=0, concat_axis=0, tiled=True
        ).astype(block_peak.dtype),
        lax.all_to_all(
            shortened(block_total), "cuts", split_axis=0, concat_axis=0, tiled=True
        ).astype(block_total.dtype),
    )
    block_out = block_out.reshape(cut_count, q_rows, head_count, head_dim)
    attended = merge_blocks(block_out, block_peak, block_total).reshape(q_rows, model_width)
    hidden = residual[0].astype(jnp.float32) + jnp.dot(
        attended, out_weight, preferred_element_type=jnp.float32
    )
    inv_rms = lax.rsqrt(jnp.mean(hidden * hidden, axis=1, keepdims=True) + 1e-06)
    normed = (hidden * inv_rms * norm_gain.astype(jnp.float32)).astype(jnp.bfloat16)
    experts = router_weight.shape[1]
    capacity = (10 * q_rows + 4 * experts - 1) // (4 * experts)
    logits = jnp.dot(normed, router_weight, preferred_element_type=jnp.float32)
    chosen = routes[0]
    onehot = (chosen[:, :, None] == jnp.arange(experts, dtype=jnp.int32)[None, None, :]).astype(
        jnp.float32
    )
    gate_values = jax.nn.sigmoid(jnp.sum(onehot * logits[:, None, :], axis=2))
    named_count = jnp.sum(onehot, axis=1)
    earlier_mask = (jnp.arange(q_rows)[:, None] > jnp.arange(q_rows)[None, :]).astype(jnp.bfloat16)
    earlier = jnp.dot(
        earlier_mask, named_count.astype(jnp.bfloat16), preferred_element_type=jnp.float32
    )
    slot_number = jnp.sum(onehot * earlier[:, None, :], axis=2)
    slot_hot = (
        slot_number[:, :, None] == jnp.arange(capacity, dtype=jnp.float32)[None, None, :]
    ).astype(jnp.float32)
    dispatch = jnp.einsum("tke,tkc->ect", onehot, slot_hot)
    buffers = jnp.einsum(
        "ect,td->ecd", dispatch.astype(jnp.bfloat16), normed, preferred_element_type=jnp.float32
    ).astype(jnp.bfloat16)
    arrived = lax.all_to_all(buffers, "req", split_axis=0, concat_axis=0, tiled=True)
    local_experts = gate_weight.shape[0]
    gathered = lax.all_gather(arrived, "cuts", axis=0, tiled=True)
    row_count = lax.axis_size("cuts") * arrived.shape[0]
    row_block = gathered.reshape(row_count, local_experts, capacity, model_width)
    expert_out = lax.psum_scatter(
        expert_part(row_block, gate_weight, up_weight, down_weight)
        .reshape(row_count, local_experts * capacity, model_width)
        .astype(jnp.bfloat16),
        "cuts",
        scatter_dimension=0,
        tiled=True,
    )
    returned = lax.all_to_all(expert_out, "req", split_axis=0, concat_axis=0, tiled=True)
    combine = jnp.einsum(
        "tke,tkc,tk->ect", onehot, slot_hot, gate_values, precision=lax.Precision.HIGHEST
    )
    gathered_back = jnp.einsum(
        "ect,ecd->td", combine, returned.astype(jnp.float32), precision=lax.Precision.HIGHEST
    )
    layer_out = hidden + gathered_back
    return layer_out.astype(jnp.bfloat16)[None]


def solution(mesh):
    return jax.shard_map(
        per_device,
        mesh=mesh,
        in_specs=(
            P("req", "cuts", None),
            P("req", "cuts", None),
            P("req", "cuts", None),
            P("req", "cuts", None),
            P("req", "cuts", None),
            P("req"),
            P(),
            P("req", "cuts", None),
            P(),
            P(),
            P(),
            P("req", "cuts", None),
            P("req", None, "cuts"),
            P("req", None, "cuts"),
            P("req", None, "cuts"),
        ),
        out_specs=P("req", "cuts", None),
        check_vma=False,
    )
```

profile of v0, /device:TPU:97, one launch (start us, length us, event | category | flops | bytes accessed | tf_op | source)
XLA Modules:
  0.0 969.2 jit_solution(8223163654308807281)
XLA Ops:
  17.1 10.8 %convert_add_fusion = s32[2048,384]{0,1:T(8,128)} fusion(s32[384]{0:T(512)S(1)} %pad_add_fusion, s32[2048]{0:T(1024)S(1)} %iota_add_fusion), kind=kLoop, calls=%fused_computation.63 | loop fusion | flops 73924608 | bytes 3155456 | tf_op jit(solution)/shard_map/add | solution.py:38
  27.9 31.0 %all-gather.6.cloned.1.call-done = bf16[1,2048,1024]{1,2,0:T(8,128)(2,1)} async-done(((bf16[1,128,1024]{1,2,0:T(8,128)(2,1)}), bf16[1,2048,1024]{1,2,0:T(8,128)(2,1)}) %all-gather.6.cloned.1.call-update) | async-done | bytes 4194320 | tf_op jit(solution)/shard_map/all_gather | solution.py:128
  58.9 562.9 %while.15 = (s32[]{:T(128)}, bf16[16,2048,64]{1,2,0:T(8,128)(2,1)}, bf16[16,2048]{1,0:T(8,128)(2,1)S(1)}, bf16[16,2048]{1,0:T(8,128)(2,1)S(1)}, bf16[16,2048,64]...) while((s32[]{:T(128)}, bf16[16,2048,64]{1,2,0:T(8,128)(2,1)}, ...), condition=%wide.region_3.4_spmd.clone, body=%wide.region_0.3_spmd.clone.sunk | while | flops 270792704 | bytes 13345049 | solution.py:78
  61.0 29.3 %fusion.139 = (f32[2048]{0:T(1024)S(1)}, f32[2048,384]{0,1:T(8,128)S(1)}) fusion(f32[]{:T(128)} %bitcast.298, f32[]{:T(128)} %bitcast.299, f32[]{:T(128)} %bitcast.300, f32[]{:T(128)} %bitcast.301, f32[]{:T(128)} %bitcast.302, f32[]{:T(128)} %bitcast.303, f32[]{:T(128)} %bitcast.304, f32[]{:T(128)} %bitcast.305, f32[]{:T(128)} %bitcast.306, ...), kind=kOutput, calls=%fused_computation.158.clone.1 | convolution fusion | flops 162002944 | bytes 6638464 | tf_op jit(solution)/shard_map/while/body/eval_jaxpr/dot_general | solution.py:56
  96.2 29.3 %fusion.139 = (f32[2048]{0:T(1024)S(1)}, f32[2048,384]{0,1:T(8,128)S(1)}) fusion(f32[]{:T(128)} %bitcast.298, f32[]{:T(128)} %bitcast.299, f32[]{:T(128)} %bitcast.300, f32[]{:T(128)} %bitcast.301, f32[]{:T(128)} %bitcast.302, f32[]{:T(128)} %bitcast.303, f32[]{:T(128)} %bitcast.304, f32[]{:T(128)} %bitcast.305, f32[]{:T(128)} %bitcast.306, ...), kind=kOutput, calls=%fused_computation.158.clone.1 | convolution fusion | flops 162002944 | bytes 6638464 | tf_op jit(solution)/shard_map/while/body/eval_jaxpr/dot_general | solution.py:56
  131.4 29.3 %fusion.139 = (f32[2048]{0:T(1024)S(1)}, f32[2048,384]{0,1:T(8,128)S(1)}) fusion(f32[]{:T(128)} %bitcast.298, f32[]{:T(128)} %bitcast.299, f32[]{:T(128)} %bitcast.300, f32[]{:T(128)} %bitcast.301, f32[]{:T(128)} %bitcast.302, f32[]{:T(128)} %bitcast.303, f32[]{:T(128)} %bitcast.304, f32[]{:T(128)} %bitcast.305, f32[]{:T(128)} %bitcast.306, ...), kind=kOutput, calls=%fused_computation.158.clone.1 | convolution fusion | flops 162002944 | bytes 6638464 | tf_op jit(solution)/shard_map/while/body/eval_jaxpr/dot_general | solution.py:56
  166.6 29.3 %fusion.139 = (f32[2048]{0:T(1024)S(1)}, f32[2048,384]{0,1:T(8,128)S(1)}) fusion(f32[]{:T(128)} %bitcast.298, f32[]{:T(128)} %bitcast.299, f32[]{:T(128)} %bitcast.300, f32[]{:T(128)} %bitcast.301, f32[]{:T(128)} %bitcast.302, f32[]{:T(128)} %bitcast.303, f32[]{:T(128)} %bitcast.304, f32[]{:T(128)} %bitcast.305, f32[]{:T(128)} %bitcast.306, ...), kind=kOutput, calls=%fused_computation.158.clone.1 | convolution fusion | flops 162002944 | bytes 6638464 | tf_op jit(solution)/shard_map/while/body/eval_jaxpr/dot_general | solution.py:56
  201.8 29.3 %fusion.139 = (f32[2048]{0:T(1024)S(1)}, f32[2048,384]{0,1:T(8,128)S(1)}) fusion(f32[]{:T(128)} %bitcast.298, f32[]{:T(128)} %bitcast.299, f32[]{:T(128)} %bitcast.300, f32[]{:T(128)} %bitcast.301, f32[]{:T(128)} %bitcast.302, f32[]{:T(128)} %bitcast.303, f32[]{:T(128)} %bitcast.304, f32[]{:T(128)} %bitcast.305, f32[]{:T(128)} %bitcast.306, ...), kind=kOutput, calls=%fused_computation.158.clone.1 | convolution fusion | flops 162002944 | bytes 6638464 | tf_op jit(solution)/shard_map/while/body/eval_jaxpr/dot_general | solution.py:56
  236.9 29.3 %fusion.139 = (f32[2048]{0:T(1024)S(1)}, f32[2048,384]{0,1:T(8,128)S(1)}) fusion(f32[]{:T(128)} %bitcast.298, f32[]{:T(128)} %bitcast.299, f32[]{:T(128)} %bitcast.300, f32[]{:T(128)} %bitcast.301, f32[]{:T(128)} %bitcast.302, f32[]{:T(128)} %bitcast.303, f32[]{:T(128)} %bitcast.304, f32[]{:T(128)} %bitcast.305, f32[]{:T(128)} %bitcast.306, ...), kind=kOutput, calls=%fused_computation.158.clone.1 | convolution fusion | flops 162002944 | bytes 6638464 | tf_op jit(solution)/shard_map/while/body/eval_jaxpr/dot_general | solution.py:56
  272.1 29.3 %fusion.139 = (f32[2048]{0:T(1024)S(1)}, f32[2048,384]{0,1:T(8,128)S(1)}) fusion(f32[]{:T(128)} %bitcast.298, f32[]{:T(128)} %bitcast.299, f32[]{:T(128)} %bitcast.300, f32[]{:T(128)} %bitcast.301, f32[]{:T(128)} %bitcast.302, f32[]{:T(128)} %bitcast.303, f32[]{:T(128)} %bitcast.304, f32[]{:T(128)} %bitcast.305, f32[]{:T(128)} %bitcast.306, ...), kind=kOutput, calls=%fused_computation.158.clone.1 | convolution fusion | flops 162002944 | bytes 6638464 | tf_op jit(solution)/shard_map/while/body/eval_jaxpr/dot_general | solution.py:56
  307.3 29.3 %fusion.139 = (f32[2048]{0:T(1024)S(1)}, f32[2048,384]{0,1:T(8,128)S(1)}) fusion(f32[]{:T(128)} %bitcast.298, f32[]{:T(128)} %bitcast.299, f32[]{:T(128)} %bitcast.300, f32[]{:T(128)} %bitcast.301, f32[]{:T(128)} %bitcast.302, f32[]{:T(128)} %bitcast.303, f32[]{:T(128)} %bitcast.304, f32[]{:T(128)} %bitcast.305, f32[]{:T(128)} %bitcast.306, ...), kind=kOutput, calls=%fused_computation.158.clone.1 | convolution fusion | flops 162002944 | bytes 6638464 | tf_op jit(solution)/shard_map/while/body/eval_jaxpr/dot_general | solution.py:56
  342.5 29.3 %fusion.139 = (f32[2048]{0:T(1024)S(1)}, f32[2048,384]{0,1:T(8,128)S(1)}) fusion(f32[]{:T(128)} %bitcast.298, f32[]{:T(128)} %bitcast.299, f32[]{:T(128)} %bitcast.300, f32[]{:T(128)} %bitcast.301, f32[]{:T(128)} %bitcast.302, f32[]{:T(128)} %bitcast.303, f32[]{:T(128)} %bitcast.304, f32[]{:T(128)} %bitcast.305, f32[]{:T(128)} %bitcast.306, ...), kind=kOutput, calls=%fused_computation.158.clone.1 | convolution fusion | flops 162002944 | bytes 6638464 | tf_op jit(solution)/shard_map/while/body/eval_jaxpr/dot_general | solution.py:56
  377.7 29.3 %fusion.139 = (f32[2048]{0:T(1024)S(1)}, f32[2048,384]{0,1:T(8,128)S(1)}) fusion(f32[]{:T(128)} %bitcast.298, f32[]{:T(128)} %bitcast.299, f32[]{:T(128)} %bitcast.300, f32[]{:T(128)} %bitcast.301, f32[]{:T(128)} %bitcast.302, f32[]{:T(128)} %bitcast.303, f32[]{:T(128)} %bitcast.304, f32[]{:T(128)} %bitcast.305, f32[]{:T(128)} %bitcast.306, ...), kind=kOutput, calls=%fused_computation.158.clone.1 | convolution fusion | flops 162002944 | bytes 6638464 | tf_op jit(solution)/shard_map/while/body/eval_jaxpr/dot_general | solution.py:56
  412.8 29.3 %fusion.139 = (f32[2048]{0:T(1024)S(1)}, f32[2048,384]{0,1:T(8,128)S(1)}) fusion(f32[]{:T(128)} %bitcast.298, f32[]{:T(128)} %bitcast.299, f32[]{:T(128)} %bitcast.300, f32[]{:T(128)} %bitcast.301, f32[]{:T(128)} %bitcast.302, f32[]{:T(128)} %bitcast.303, f32[]{:T(128)} %bitcast.304, f32[]{:T(128)} %bitcast.305, f32[]{:T(128)} %bitcast.306, ...), kind=kOutput, calls=%fused_computation.158.clone.1 | convolution fusion | flops 162002944 | bytes 6638464 | tf_op jit(solution)/shard_map/while/body/eval_jaxpr/dot_general | solution.py:56
  448.0 29.3 %fusion.139 = (f32[2048]{0:T(1024)S(1)}, f32[2048,384]{0,1:T(8,128)S(1)}) fusion(f32[]{:T(128)} %bitcast.298, f32[]{:T(128)} %bitcast.299, f32[]{:T(128)} %bitcast.300, f32[]{:T(128)} %bitcast.301, f32[]{:T(128)} %bitcast.302, f32[]{:T(128)} %bitcast.303, f32[]{:T(128)} %bitcast.304, f32[]{:T(128)} %bitcast.305, f32[]{:T(128)} %bitcast.306, ...), kind=kOutput, calls=%fused_computation.158.clone.1 | convolution fusion | flops 162002944 | bytes 6638464 | tf_op jit(solution)/shard_map/while/body/eval_jaxpr/dot_general | solution.py:56
  483.2 29.3 %fusion.139 = (f32[2048]{0:T(1024)S(1)}, f32[2048,384]{0,1:T(8,128)S(1)}) fusion(f32[]{:T(128)} %bitcast.298, f32[]{:T(128)} %bitcast.299, f32[]{:T(128)} %bitcast.300, f32[]{:T(128)} %bitcast.301, f32[]{:T(128)} %bitcast.302, f32[]{:T(128)} %bitcast.303, f32[]{:T(128)} %bitcast.304, f32[]{:T(128)} %bitcast.305, f32[]{:T(128)} %bitcast.306, ...), kind=kOutput, calls=%fused_computation.158.clone.1 | convolution fusion | flops 162002944 | bytes 6638464 | tf_op jit(solution)/shard_map/while/body/eval_jaxpr/dot_general | solution.py:56
  518.4 29.3 %fusion.139 = (f32[2048]{0:T(1024)S(1)}, f32[2048,384]{0,1:T(8,128)S(1)}) fusion(f32[]{:T(128)} %bitcast.298, f32[]{:T(128)} %bitcast.299, f32[]{:T(128)} %bitcast.300, f32[]{:T(128)} %bitcast.301, f32[]{:T(128)} %bitcast.302, f32[]{:T(128)} %bitcast.303, f32[]{:T(128)} %bitcast.304, f32[]{:T(128)} %bitcast.305, f32[]{:T(128)} %bitcast.306, ...), kind=kOutput, calls=%fused_computation.158.clone.1 | convolution fusion | flops 162002944 | bytes 6638464 | tf_op jit(solution)/shard_map/while/body/eval_jaxpr/dot_general | solution.py:56
  553.6 29.3 %fusion.139 = (f32[2048]{0:T(1024)S(1)}, f32[2048,384]{0,1:T(8,128)S(1)}) fusion(f32[]{:T(128)} %bitcast.298, f32[]{:T(128)} %bitcast.299, f32[]{:T(128)} %bitcast.300, f32[]{:T(128)} %bitcast.301, f32[]{:T(128)} %bitcast.302, f32[]{:T(128)} %bitcast.303, f32[]{:T(128)} %bitcast.304, f32[]{:T(128)} %bitcast.305, f32[]{:T(128)} %bitcast.306, ...), kind=kOutput, calls=%fused_computation.158.clone.1 | convolution fusion | flops 162002944 | bytes 6638464 | tf_op jit(solution)/shard_map/while/body/eval_jaxpr/dot_general | solution.py:56
  588.7 29.3 %fusion.139 = (f32[2048]{0:T(1024)S(1)}, f32[2048,384]{0,1:T(8,128)S(1)}) fusion(f32[]{:T(128)} %bitcast.298, f32[]{:T(128)} %bitcast.299, f32[]{:T(128)} %bitcast.300, f32[]{:T(128)} %bitcast.301, f32[]{:T(128)} %bitcast.302, f32[]{:T(128)} %bitcast.303, f32[]{:T(128)} %bitcast.304, f32[]{:T(128)} %bitcast.305, f32[]{:T(128)} %bitcast.306, ...), kind=kOutput, calls=%fused_computation.158.clone.1 | convolution fusion | flops 162002944 | bytes 6638464 | tf_op jit(solution)/shard_map/while/body/eval_jaxpr/dot_general | solution.py:56
  654.6 92.8 %all-to-all-done.2 = bf16[16,128,1024]{1,2,0:T(8,128)(2,1)} async-done(((bf16[16,128,1024]{1,2,0:T(8,128)(2,1)}), bf16[16,128,1024]{1,2,0:T(8,128)(2,1)}, u32[]{:S(2)}, u32[]{:S(2)}) %all-to-all-start.2) | async-done | bytes 4194336 | tf_op jit(solution)/shard_map/all_to_all | solution.py:136
  753.3 19.7 %all_to_all.25 = bf16[16,20,1024]{2,1,0:T(8,128)(2,1)S(1)} all-to-all(bf16[16,20,1024]{2,1,0:T(8,128)(2,1)S(1)} %convolution_convert_fusion.1), channel_id=1, replica_groups=mesh['req'=16,'cuts'=16] {'req'}, dimensions={0} | all-to-all | bytes 1310720 | tf_op jit(solution)/shard_map/all_to_all | solution.py:175
  774.4 62.7 %all-gather.4.cloned.1.call-done = bf16[256,20,1024]{2,0,1:T(8,128)(2,1)} async-done(((bf16[16,20,1024]{2,0,1:T(8,128)(2,1)}), bf16[256,20,1024]{2,0,1:T(8,128)(2,1)}) %all-gather.4.cloned.1.call-update) | async-done | bytes 10485776 | tf_op jit(solution)/shard_map/all_gather | solution.py:177
  846.4 18.0 %convolution_convert_fusion = bf16[256,20,1024]{2,0,1:T(8,128)(2,1)} fusion(f32[256,20,176]{0,2,1:T(8,128)} %fusion.95, bf16[256,20,1024]{2,0,1:T(8,128)(2,1)} %all-gather.4.cloned.1.call-done, bf16[1,1024,176]{1,2,0:T(8,128)(2,1)S(1)} %copy-done.7, bf16[1,1024,176]{1,2,0:T(8,128)(2,1)} %param.30), kind=kOutput, calls=%fused_computation.52 | convolution fusion | flops 3705241600 | bytes 25296896 | tf_op jit(solution)/shard_map/necf,edf->necd/dot_general | solution.py:96
  864.5 73.4 %reduce-scatter.2.cloned.1.call-done = bf16[16,20,1024]{2,0,1:T(8,128)(2,1)} async-done(((bf16[256,20,1024]{2,0,1:T(8,128)(2,1)}), bf16[16,20,1024]{2,0,1:T(8,128)(2,1)}) %reduce-scatter.2.cloned.1.call-update) | async-done | bytes 655376 | tf_op jit(solution)/shard_map/reduce_scatter | solution.py:180
  (198 shorter events, 177.2 us)
Async XLA Ops:
  6.5 744.0 %copy-start = (bf16[1024,1024]{1,0:T(8,128)(2,1)S(1)}, bf16[1024,1024]{1,0:T(8,128)(2,1)}, u32[]{:S(2)}) copy-start(bf16[1024,1024]{1,0:T(8,128)(2,1)} %param.25) | copy-start | bytes 6291460
  6.5 52.4 %all-gather.6.cloned.1.call-start = ((), (), s32[]{:S(2)}) async-start(), calls=%async_computation.8 | async-start | bytes 4456448 | tf_op jit(solution)/shard_map/all_gather | solution.py:128
  622.5 11.0 %all-to-all-start.1 = ((bf16[16,128,16]{1,2,0:T(8,128)(2,1)}), bf16[16,128,16]{1,2,0:T(8,128)(2,1)S(1)}, u32[]{:S(2)}, u32[]{:S(2)}) async-start(bf16[16,128,16]{1,2,0:T(8,128)(2,1)} %copy_bitcast_fusion), calls=%async_computation.1 | async-start | bytes 131072 | tf_op jit(solution)/shard_map/all_to_all | solution.py:143
  633.5 12.9 %all-to-all-start = ((bf16[16,128,16]{1,2,0:T(8,128)(2,1)}), bf16[16,128,16]{1,2,0:T(8,128)(2,1)S(1)}, u32[]{:S(2)}, u32[]{:S(2)}) async-start(bf16[16,128,16]{1,2,0:T(8,128)(2,1)} %copy_bitcast_fusion.1), calls=%async_computation | async-start | bytes 131072 | tf_op jit(solution)/shard_map/all_to_all | solution.py:140
  646.3 7.6 copy-start.5
  646.3 7.6 copy-start.6
  646.3 101.1 %all-to-all-start.2 = ((bf16[16,128,1024]{1,2,0:T(8,128)(2,1)}), bf16[16,128,1024]{1,2,0:T(8,128)(2,1)}, u32[]{:S(2)}, u32[]{:S(2)}) async-start(bf16[16,128,1024]{1,2,0:T(8,128)(2,1)} %copy.112), calls=%async_computation.2 | async-start | bytes 8388608 | tf_op jit(solution)/shard_map/all_to_all | solution.py:136
  653.7 96.9 %copy-start.2 = (bf16[1,128,1024]{2,1,0:T(8,128)(2,1)S(1)}, bf16[1,128,1024]{2,1,0:T(8,128)(2,1)}, u32[]{:S(2)}) copy-start(bf16[1,128,1024]{2,1,0:T(8,128)(2,1)} %param.24) | copy-start | bytes 786436
  653.7 183.3 %all-gather.4.cloned.1.call-start = ((), (), s32[]{:S(2)}) async-start(), calls=%async_computation.6 | async-start | bytes 11141120 | tf_op jit(solution)/shard_map/all_gather | solution.py:177
  750.5 0.8 copy-start.4
  752.0 22.2 %copy-start.3 = (f32[128,2]{1,0:T(8,128)}, f32[128,2]{1,0:T(8,128)S(1)}, u32[]{:S(2)}) copy-start(f32[128,2]{1,0:T(8,128)S(1)} %get-tuple-element.164) | copy-start | bytes 3076
  753.3 83.7 %copy-start.1 = (bf16[1,1024,176]{1,2,0:T(8,128)(2,1)S(1)}, bf16[1,1024,176]{1,2,0:T(8,128)(2,1)}, u32[]{:S(2)}) copy-start(bf16[1,1024,176]{1,2,0:T(8,128)(2,1)} %param.29) | copy-start | bytes 1081348
  774.3 72.1 %copy-start.7 = (bf16[1,1024,176]{1,2,0:T(8,128)(2,1)S(1)}, bf16[1,1024,176]{1,2,0:T(8,128)(2,1)}, u32[]{:S(2)}) copy-start(bf16[1,1024,176]{1,2,0:T(8,128)(2,1)} %param.31) | copy-start | bytes 1081348
  774.3 163.6 %reduce-scatter.2.cloned.1.call-start = ((), (), s32[]{:S(2)}) async-start(), calls=%async_computation.7 | async-start | bytes 11141120 | tf_op jit(solution)/shard_map/reduce_scatter | solution.py:180
  940.2 19.2 %all-to-all-start.4 = ((bf16[16,20,1024]{2,1,0:T(8,128)(2,1)}), bf16[16,20,1024]{2,1,0:T(8,128)(2,1)S(1)}, u32[]{:S(2)}, u32[]{:S(2)}) async-start(bf16[16,20,1024]{2,1,0:T(8,128)(2,1)} %copy.120), calls=%async_computation.5 | async-start | bytes 1572864 | tf_op jit(solution)/shard_map/all_to_all | solution.py:188
Sparse Core Ops, SparseCore 0:
  9.1 49.7 all-gather.5
  774.4 62.5 all-gather.3
  864.6 73.2 reduce-scatter.1
where the time goes:
time: 976 us; the launch traced here: 969 us
  matrix products  545 us (56%)
  waiting for transfers between devices  274 us (28%)
  local copies, waits for them, and re-layouts  56 us (6%)
  other arithmetic  33 us (3%)
  starting transfers between devices  26.5 us (3%)
  blocking collectives  19.7 us (2%)
  between operations  14 us (1%)
    dot_general x16, matrix products, head_partial(): lax.dot_general(query_rows, key_rows, (((1,), (1,)), ((), ())), preferred...  469 us
    all_to_all x1, waiting for transfers between devices, per_device(): lax.all_to_all(shortened(block_out), 'cuts', split_axis=0, concat_axis=0,...  92.8 us
    reduce_scatter x1, waiting for transfers between devices, per_device(): lax.psum_scatter(expert_part(row_block, gate_weight, up_weight, down_weig...  73.4 us
    all_gather x1, waiting for transfers between devices, per_device(): gathered = lax.all_gather(arrived, 'cuts', axis=0, tiled=True)  62.7 us
    dot_general x16, matrix products, head_partial(): jnp.dot(weights.astype(jnp.bfloat16), value_rows, preferred_element_type=...  40.8 us
    all_gather x1, waiting for transfers between devices, per_device(): every_query = lax.all_gather(queries[0], 'cuts', axis=0, tiled=True)  31 us
    gather x32, local copies, waits for them, and re-layouts, head_partial(): masked = jnp.where(visible, scores + jnp.take(bias_table, bucket), -1e+30)  22.6 us
    all_to_all x1, blocking collectives, per_device(): lax.all_to_all(buffers, 'req', split_axis=0, concat_axis=0, tiled=True)  19.7 us
  transfers between devices with their start and end apart: 7, of which 6 were waited for; matrix products, arithmetic and copies ran while one was open for 3% of the time, Pallas kernels for 0%

commit v1 on v0

--- a/solution.py
+++ b/solution.py
@@ -125,7 +125,9 @@
     query_total = q_rows * cut_count
     local_keys = jnp.concatenate([cache_keys[0], new_keys[0]], axis=0)
     local_values = jnp.concatenate([cache_values[0], new_values[0]], axis=0)
-    every_query = lax.all_gather(queries[0], "cuts", axis=0, tiled=True)
+    every_query = jnp.concatenate(
+        lax.all_to_all(jnp.stack([queries[0]] * lax.axis_size("cuts")), "cuts", 0, 0), axis=0
+    )
     visible, bucket = block_masks(cut_index, length, cache_rows, q_rows, query_total, bucket_count)
     block_out, block_peak, block_total = block_partials(
         every_query, local_keys, local_values, relative_bias, visible, bucket

time: 976 us -> 1050 us (1.076)
  waiting for transfers between devices: 274 us -> 319 us
  local copies, waits for them, and re-layouts: 56 us -> 70.4 us
    all_to_all x0 -> x1, waiting for transfers between devices: none -> 76.4 us  [per_device(): lax.all_to_all(jnp.stack([queries[0]] * lax.axis_size('cuts')), 'cuts', 0...]
    all_gather x1 -> x0, waiting for transfers between devices: 31 us -> none  [per_device(): every_query = lax.all_gather(queries[0], 'cuts', axis=0, tiled=True)]
    another operation x0 -> x3, local copies, waits for them, and re-layouts: none -> 11.3 us  [the longest x1 7.28 us: block_partials(): query_rows.reshape(query_rows.shape[0], head_count, head_dim)]
where the time goes in v1:
time: 1050 us; the launch traced here: 1040 us
  matrix products  550 us (52%)
  waiting for transfers between devices  319 us (30%)
  local copies, waits for them, and re-layouts  70.4 us (7%)
  starting transfers between devices  33.8 us (3%)
  other arithmetic  33 us (3%)
  blocking collectives  20 us (2%)
  between operations  14.4 us (1%)
    dot_general x16, matrix products, head_partial(): lax.dot_general(query_rows, key_rows, (((1,), (1,)), ((), ())), preferred...  473 us
    all_to_all x1, waiting for transfers between devices, per_device(): lax.all_to_all(shortened(block_out), 'cuts', split_axis=0, concat_axis=0,...  93 us
    all_to_all x1, waiting for transfers between devices, per_device(): lax.all_to_all(jnp.stack([queries[0]] * lax.axis_size('cuts')), 'cuts', 0...  76.4 us
    reduce_scatter x1, waiting for transfers between devices, per_device(): lax.psum_scatter(expert_part(row_block, gate_weight, up_weight, down_weig...  73.4 us
    all_gather x1, waiting for transfers between devices, per_device(): gathered = lax.all_gather(arrived, 'cuts', axis=0, tiled=True)  62.5 us
    dot_general x16, matrix products, head_partial(): jnp.dot(weights.astype(jnp.bfloat16), value_rows, preferred_element_type=...  40.8 us
    gather x32, local copies, waits for them, and re-layouts, head_partial(): masked = jnp.where(visible, scores + jnp.take(bias_table, bucket), -1e+30)  22.8 us
  transfers between devices with their start and end apart: 7, of which 6 were waited for; matrix products, arithmetic and copies ran while one was open for 3% of the time, Pallas kernels for 0%

profile of v1, /device:TPU:97, one launch (start us, length us, event | category | flops | bytes accessed | tf_op | source)
XLA Modules:
  0.0 1041.5 jit_solution(15074535585873083652)
XLA Ops:
  25.2 10.9 %convert_add_fusion = s32[2048,384]{0,1:T(8,128)} fusion(s32[384]{0:T(512)S(1)} %pad_add_fusion, s32[2048]{0:T(1024)S(1)} %iota_add_fusion), kind=kLoop, calls=%fused_computation.63 | loop fusion | flops 73924608 | bytes 3155456 | tf_op jit(solution)/shard_map/add | solution.py:38
  36.0 76.4 %all-to-all-done = bf16[16,128,1024]{1,2,0:T(8,128)(2,1)} async-done(((bf16[16,128,1024]{1,2,0:T(8,128)(2,1)}), bf16[16,128,1024]{1,2,0:T(8,128)(2,1)}, u32[]{:S(2)}, u32[]{:S(2)}) %all-to-all-start) | async-done | bytes 4194336 | tf_op jit(solution)/shard_map/all_to_all | solution.py:129
  126.5 567.8 %while.15 = (s32[]{:T(128)}, bf16[16,2048,64]{1,2,0:T(8,128)(2,1)}, bf16[16,2048]{1,0:T(8,128)(2,1)S(1)}, bf16[16,2048]{1,0:T(8,128)(2,1)S(1)}, bf16[16,2048,64]...) while((s32[]{:T(128)}, bf16[16,2048,64]{1,2,0:T(8,128)(2,1)}, ...), condition=%wide.region_3.4_spmd.clone, body=%wide.region_0.3_spmd.clone.sunk | while | flops 270792704 | bytes 13345049 | solution.py:78
  128.6 29.6 %fusion.139 = (f32[2048]{0:T(1024)S(1)}, f32[2048,384]{0,1:T(8,128)S(1)}) fusion(f32[]{:T(128)} %bitcast.299, f32[]{:T(128)} %bitcast.300, f32[]{:T(128)} %bitcast.301, f32[]{:T(128)} %bitcast.302, f32[]{:T(128)} %bitcast.303, f32[]{:T(128)} %bitcast.304, f32[]{:T(128)} %bitcast.305, f32[]{:T(128)} %bitcast.306, f32[]{:T(128)} %bitcast.307, ...), kind=kOutput, calls=%fused_computation.158.clone.1 | convolution fusion | flops 162002944 | bytes 6638464 | tf_op jit(solution)/shard_map/while/body/eval_jaxpr/dot_general | solution.py:56
  164.1 29.6 %fusion.139 = (f32[2048]{0:T(1024)S(1)}, f32[2048,384]{0,1:T(8,128)S(1)}) fusion(f32[]{:T(128)} %bitcast.299, f32[]{:T(128)} %bitcast.300, f32[]{:T(128)} %bitcast.301, f32[]{:T(128)} %bitcast.302, f32[]{:T(128)} %bitcast.303, f32[]{:T(128)} %bitcast.304, f32[]{:T(128)} %bitcast.305, f32[]{:T(128)} %bitcast.306, f32[]{:T(128)} %bitcast.307, ...), kind=kOutput, calls=%fused_computation.158.clone.1 | convolution fusion | flops 162002944 | bytes 6638464 | tf_op jit(solution)/shard_map/while/body/eval_jaxpr/dot_general | solution.py:56
  199.6 29.6 %fusion.139 = (f32[2048]{0:T(1024)S(1)}, f32[2048,384]{0,1:T(8,128)S(1)}) fusion(f32[]{:T(128)} %bitcast.299, f32[]{:T(128)} %bitcast.300, f32[]{:T(128)} %bitcast.301, f32[]{:T(128)} %bitcast.302, f32[]{:T(128)} %bitcast.303, f32[]{:T(128)} %bitcast.304, f32[]{:T(128)} %bitcast.305, f32[]{:T(128)} %bitcast.306, f32[]{:T(128)} %bitcast.307, ...), kind=kOutput, calls=%fused_computation.158.clone.1 | convolution fusion | flops 162002944 | bytes 6638464 | tf_op jit(solution)/shard_map/while/body/eval_jaxpr/dot_general | solution.py:56
  235.1 29.6 %fusion.139 = (f32[2048]{0:T(1024)S(1)}, f32[2048,384]{0,1:T(8,128)S(1)}) fusion(f32[]{:T(128)} %bitcast.299, f32[]{:T(128)} %bitcast.300, f32[]{:T(128)} %bitcast.301, f32[]{:T(128)} %bitcast.302, f32[]{:T(128)} %bitcast.303, f32[]{:T(128)} %bitcast.304, f32[]{:T(128)} %bitcast.305, f32[]{:T(128)} %bitcast.306, f32[]{:T(128)} %bitcast.307, ...), kind=kOutput, calls=%fused_computation.158.clone.1 | convolution fusion | flops 162002944 | bytes 6638464 | tf_op jit(solution)/shard_map/while/body/eval_jaxpr/dot_general | solution.py:56
  270.6 29.6 %fusion.139 = (f32[2048]{0:T(1024)S(1)}, f32[2048,384]{0,1:T(8,128)S(1)}) fusion(f32[]{:T(128)} %bitcast.299, f32[]{:T(128)} %bitcast.300, f32[]{:T(128)} %bitcast.301, f32[]{:T(128)} %bitcast.302, f32[]{:T(128)} %bitcast.303, f32[]{:T(128)} %bitcast.304, f32[]{:T(128)} %bitcast.305, f32[]{:T(128)} %bitcast.306, f32[]{:T(128)} %bitcast.307, ...), kind=kOutput, calls=%fused_computation.158.clone.1 | convolution fusion | flops 162002944 | bytes 6638464 | tf_op jit(solution)/shard_map/while/body/eval_jaxpr/dot_general | solution.py:56
  306.1 29.6 %fusion.139 = (f32[2048]{0:T(1024)S(1)}, f32[2048,384]{0,1:T(8,128)S(1)}) fusion(f32[]{:T(128)} %bitcast.299, f32[]{:T(128)} %bitcast.300, f32[]{:T(128)} %bitcast.301, f32[]{:T(128)} %bitcast.302, f32[]{:T(128)} %bitcast.303, f32[]{:T(128)} %bitcast.304, f32[]{:T(128)} %bitcast.305, f32[]{:T(128)} %bitcast.306, f32[]{:T(128)} %bitcast.307, ...), kind=kOutput, calls=%fused_computation.158.clone.1 | convolution fusion | flops 162002944 | bytes 6638464 | tf_op jit(solution)/shard_map/while/body/eval_jaxpr/dot_general | solution.py:56
  341.6 29.6 %fusion.139 = (f32[2048]{0:T(1024)S(1)}, f32[2048,384]{0,1:T(8,128)S(1)}) fusion(f32[]{:T(128)} %bitcast.299, f32[]{:T(128)} %bitcast.300, f32[]{:T(128)} %bitcast.301, f32[]{:T(128)} %bitcast.302, f32[]{:T(128)} %bitcast.303, f32[]{:T(128)} %bitcast.304, f32[]{:T(128)} %bitcast.305, f32[]{:T(128)} %bitcast.306, f32[]{:T(128)} %bitcast.307, ...), kind=kOutput, calls=%fused_computation.158.clone.1 | convolution fusion | flops 162002944 | bytes 6638464 | tf_op jit(solution)/shard_map/while/body/eval_jaxpr/dot_general | solution.py:56
  377.0 29.6 %fusion.139 = (f32[2048]{0:T(1024)S(1)}, f32[2048,384]{0,1:T(8,128)S(1)}) fusion(f32[]{:T(128)} %bitcast.299, f32[]{:T(128)} %bitcast.300, f32[]{:T(128)} %bitcast.301, f32[]{:T(128)} %bitcast.302, f32[]{:T(128)} %bitcast.303, f32[]{:T(128)} %bitcast.304, f32[]{:T(128)} %bitcast.305, f32[]{:T(128)} %bitcast.306, f32[]{:T(128)} %bitcast.307, ...), kind=kOutput, calls=%fused_computation.158.clone.1 | convolution fusion | flops 162002944 | bytes 6638464 | tf_op jit(solution)/shard_map/while/body/eval_jaxpr/dot_general | solution.py:56
  412.5 29.6 %fusion.139 = (f32[2048]{0:T(1024)S(1)}, f32[2048,384]{0,1:T(8,128)S(1)}) fusion(f32[]{:T(128)} %bitcast.299, f32[]{:T(128)} %bitcast.300, f32[]{:T(128)} %bitcast.301, f32[]{:T(128)} %bitcast.302, f32[]{:T(128)} %bitcast.303, f32[]{:T(128)} %bitcast.304, f32[]{:T(128)} %bitcast.305, f32[]{:T(128)} %bitcast.306, f32[]{:T(128)} %bitcast.307, ...), kind=kOutput, calls=%fused_computation.158.clone.1 | convolution fusion | flops 162002944 | bytes 6638464 | tf_op jit(solution)/shard_map/while/body/eval_jaxpr/dot_general | solution.py:56
  448.0 29.6 %fusion.139 = (f32[2048]{0:T(1024)S(1)}, f32[2048,384]{0,1:T(8,128)S(1)}) fusion(f32[]{:T(128)} %bitcast.299, f32[]{:T(128)} %bitcast.300, f32[]{:T(128)} %bitcast.301, f32[]{:T(128)} %bitcast.302, f32[]{:T(128)} %bitcast.303, f32[]{:T(128)} %bitcast.304, f32[]{:T(128)} %bitcast.305, f32[]{:T(128)} %bitcast.306, f32[]{:T(128)} %bitcast.307, ...), kind=kOutput, calls=%fused_computation.158.clone.1 | convolution fusion | flops 162002944 | bytes 6638464 | tf_op jit(solution)/shard_map/while/body/eval_jaxpr/dot_general | solution.py:56
  483.5 29.6 %fusion.139 = (f32[2048]{0:T(1024)S(1)}, f32[2048,384]{0,1:T(8,128)S(1)}) fusion(f32[]{:T(128)} %bitcast.299, f32[]{:T(128)} %bitcast.300, f32[]{:T(128)} %bitcast.301, f32[]{:T(128)} %bitcast.302, f32[]{:T(128)} %bitcast.303, f32[]{:T(128)} %bitcast.304, f32[]{:T(128)} %bitcast.305, f32[]{:T(128)} %bitcast.306, f32[]{:T(128)} %bitcast.307, ...), kind=kOutput, calls=%fused_computation.158.clone.1 | convolution fusion | flops 162002944 | bytes 6638464 | tf_op jit(solution)/shard_map/while/body/eval_jaxpr/dot_general | solution.py:56
  519.0 29.6 %fusion.139 = (f32[2048]{0:T(1024)S(1)}, f32[2048,384]{0,1:T(8,128)S(1)}) fusion(f32[]{:T(128)} %bitcast.299, f32[]{:T(128)} %bitcast.300, f32[]{:T(128)} %bitcast.301, f32[]{:T(128)} %bitcast.302, f32[]{:T(128)} %bitcast.303, f32[]{:T(128)} %bitcast.304, f32[]{:T(128)} %bitcast.305, f32[]{:T(128)} %bitcast.306, f32[]{:T(128)} %bitcast.307, ...), kind=kOutput, calls=%fused_computation.158.clone.1 | convolution fusion | flops 162002944 | bytes 6638464 | tf_op jit(solution)/shard_map/while/body/eval_jaxpr/dot_general | solution.py:56
  554.5 29.6 %fusion.139 = (f32[2048]{0:T(1024)S(1)}, f32[2048,384]{0,1:T(8,128)S(1)}) fusion(f32[]{:T(128)} %bitcast.299, f32[]{:T(128)} %bitcast.300, f32[]{:T(128)} %bitcast.301, f32[]{:T(128)} %bitcast.302, f32[]{:T(128)} %bitcast.303, f32[]{:T(128)} %bitcast.304, f32[]{:T(128)} %bitcast.305, f32[]{:T(128)} %bitcast.306, f32[]{:T(128)} %bitcast.307, ...), kind=kOutput, calls=%fused_computation.158.clone.1 | convolution fusion | flops 162002944 | bytes 6638464 | tf_op jit(solution)/shard_map/while/body/eval_jaxpr/dot_general | solution.py:56
  590.0 29.6 %fusion.139 = (f32[2048]{0:T(1024)S(1)}, f32[2048,384]{0,1:T(8,128)S(1)}) fusion(f32[]{:T(128)} %bitcast.299, f32[]{:T(128)} %bitcast.300, f32[]{:T(128)} %bitcast.301, f32[]{:T(128)} %bitcast.302, f32[]{:T(128)} %bitcast.303, f32[]{:T(128)} %bitcast.304, f32[]{:T(128)} %bitcast.305, f32[]{:T(128)} %bitcast.306, f32[]{:T(128)} %bitcast.307, ...), kind=kOutput, calls=%fused_computation.158.clone.1 | convolution fusion | flops 162002944 | bytes 6638464 | tf_op jit(solution)/shard_map/while/body/eval_jaxpr/dot_general | solution.py:56
  625.5 29.6 %fusion.139 = (f32[2048]{0:T(1024)S(1)}, f32[2048,384]{0,1:T(8,128)S(1)}) fusion(f32[]{:T(128)} %bitcast.299, f32[]{:T(128)} %bitcast.300, f32[]{:T(128)} %bitcast.301, f32[]{:T(128)} %bitcast.302, f32[]{:T(128)} %bitcast.303, f32[]{:T(128)} %bitcast.304, f32[]{:T(128)} %bitcast.305, f32[]{:T(128)} %bitcast.306, f32[]{:T(128)} %bitcast.307, ...), kind=kOutput, calls=%fused_computation.158.clone.1 | convolution fusion | flops 162002944 | bytes 6638464 | tf_op jit(solution)/shard_map/while/body/eval_jaxpr/dot_general | solution.py:56
  660.9 29.6 %fusion.139 = (f32[2048]{0:T(1024)S(1)}, f32[2048,384]{0,1:T(8,128)S(1)}) fusion(f32[]{:T(128)} %bitcast.299, f32[]{:T(128)} %bitcast.300, f32[]{:T(128)} %bitcast.301, f32[]{:T(128)} %bitcast.302, f32[]{:T(128)} %bitcast.303, f32[]{:T(128)} %bitcast.304, f32[]{:T(128)} %bitcast.305, f32[]{:T(128)} %bitcast.306, f32[]{:T(128)} %bitcast.307, ...), kind=kOutput, calls=%fused_computation.158.clone.1 | convolution fusion | flops 162002944 | bytes 6638464 | tf_op jit(solution)/shard_map/while/body/eval_jaxpr/dot_general | solution.py:56
  726.2 93.0 %all-to-all-done.3 = bf16[16,128,1024]{1,2,0:T(8,128)(2,1)} async-done(((bf16[16,128,1024]{1,2,0:T(8,128)(2,1)}), bf16[16,128,1024]{1,2,0:T(8,128)(2,1)}, u32[]{:S(2)}, u32[]{:S(2)}) %all-to-all-start.3) | async-done | bytes 4194336 | tf_op jit(solution)/shard_map/all_to_all | solution.py:138
  825.1 20.0 %all_to_all.30 = bf16[16,20,1024]{2,1,0:T(8,128)(2,1)S(1)} all-to-all(bf16[16,20,1024]{2,1,0:T(8,128)(2,1)S(1)} %convolution_convert_fusion.1), channel_id=1, replica_groups=mesh['req'=16,'cuts'=16] {'req'}, dimensions={0} | all-to-all | bytes 1310720 | tf_op jit(solution)/shard_map/all_to_all | solution.py:177
  846.6 62.5 %all-gather.2.cloned.1.call-done = bf16[256,20,1024]{2,0,1:T(8,128)(2,1)} async-done(((bf16[16,20,1024]{2,0,1:T(8,128)(2,1)}), bf16[256,20,1024]{2,0,1:T(8,128)(2,1)}) %all-gather.2.cloned.1.call-update) | async-done | bytes 10485776 | tf_op jit(solution)/shard_map/all_gather | solution.py:179
  918.5 18.0 %convolution_convert_fusion = bf16[256,20,1024]{2,0,1:T(8,128)(2,1)} fusion(f32[256,20,176]{0,2,1:T(8,128)} %fusion.95, bf16[256,20,1024]{2,0,1:T(8,128)(2,1)} %all-gather.2.cloned.1.call-done, bf16[1,1024,176]{1,2,0:T(8,128)(2,1)S(1)} %copy-done.9, bf16[1,1024,176]{1,2,0:T(8,128)(2,1)} %param.30), kind=kOutput, calls=%fused_computation.52 | convolution fusion | flops 3705241600 | bytes 25296896 | tf_op jit(solution)/shard_map/necf,edf->necd/dot_general | solution.py:96
  936.5 73.4 %reduce-scatter.2.cloned.1.call-done = bf16[16,20,1024]{2,0,1:T(8,128)(2,1)} async-done(((bf16[256,20,1024]{2,0,1:T(8,128)(2,1)}), bf16[16,20,1024]{2,0,1:T(8,128)(2,1)}) %reduce-scatter.2.cloned.1.call-update) | async-done | bytes 655376 | tf_op jit(solution)/shard_map/reduce_scatter | solution.py:182
  (204 shorter events, 198.9 us)
Async XLA Ops:
  6.5 815.8 %copy-start = (bf16[1024,1024]{1,0:T(8,128)(2,1)S(1)}, bf16[1024,1024]{1,0:T(8,128)(2,1)}, u32[]{:S(2)}) copy-start(bf16[1024,1024]{1,0:T(8,128)(2,1)} %param.25) | copy-start | bytes 6291460
  10.6 8.1 copy-start.3
  10.6 8.3 copy-start.1
  10.6 101.8 %all-to-all-start = ((bf16[16,128,1024]{1,2,0:T(8,128)(2,1)}), bf16[16,128,1024]{1,2,0:T(8,128)(2,1)}, u32[]{:S(2)}, u32[]{:S(2)}) async-start(bf16[16,128,1024]{1,2,0:T(8,128)(2,1)} %stack.3), calls=%async_computation | async-start | bytes 8388608 | tf_op jit(solution)/shard_map/all_to_all | solution.py:129
  695.0 10.3 all-to-all-start.2
  705.2 12.9 %all-to-all-start.1 = ((bf16[16,128,16]{1,2,0:T(8,128)(2,1)}), bf16[16,128,16]{1,2,0:T(8,128)(2,1)S(1)}, u32[]{:S(2)}, u32[]{:S(2)}) async-start(bf16[16,128,16]{1,2,0:T(8,128)(2,1)} %copy_bitcast_fusion.1), calls=%async_computation.1 | async-start | bytes 131072 | tf_op jit(solution)/shard_map/all_to_all | solution.py:142
  718.1 7.4 copy-start.7
  718.1 7.4 copy-start.8
  718.1 101.1 %all-to-all-start.3 = ((bf16[16,128,1024]{1,2,0:T(8,128)(2,1)}), bf16[16,128,1024]{1,2,0:T(8,128)(2,1)}, u32[]{:S(2)}, u32[]{:S(2)}) async-start(bf16[16,128,1024]{1,2,0:T(8,128)(2,1)} %copy.117), calls=%async_computation.3 | async-start | bytes 8388608 | tf_op jit(solution)/shard_map/all_to_all | solution.py:138
  725.5 96.9 %copy-start.4 = (bf16[1,128,1024]{2,1,0:T(8,128)(2,1)S(1)}, bf16[1,128,1024]{2,1,0:T(8,128)(2,1)}, u32[]{:S(2)}) copy-start(bf16[1,128,1024]{2,1,0:T(8,128)(2,1)} %param.24) | copy-start | bytes 786436
  725.5 183.6 %all-gather.2.cloned.1.call-start = ((), (), s32[]{:S(2)}) async-start(), calls=%async_computation.7 | async-start | bytes 11141120 | tf_op jit(solution)/shard_map/all_gather | solution.py:179
  822.3 0.8 copy-start.6
  823.8 22.5 %copy-start.5 = (f32[128,2]{1,0:T(8,128)}, f32[128,2]{1,0:T(8,128)S(1)}, u32[]{:S(2)}) copy-start(f32[128,2]{1,0:T(8,128)S(1)} %get-tuple-element.164) | copy-start | bytes 3076
  825.1 84.0 %copy-start.2 = (bf16[1,1024,176]{1,2,0:T(8,128)(2,1)S(1)}, bf16[1,1024,176]{1,2,0:T(8,128)(2,1)}, u32[]{:S(2)}) copy-start(bf16[1,1024,176]{1,2,0:T(8,128)(2,1)} %param.29) | copy-start | bytes 1081348
  846.3 72.1 %copy-start.9 = (bf16[1,1024,176]{1,2,0:T(8,128)(2,1)S(1)}, bf16[1,1024,176]{1,2,0:T(8,128)(2,1)}, u32[]{:S(2)}) copy-start(bf16[1,1024,176]{1,2,0:T(8,128)(2,1)} %param.31) | copy-start | bytes 1081348
  846.4 163.6 %reduce-scatter.2.cloned.1.call-start = ((), (), s32[]{:S(2)}) async-start(), calls=%async_computation.8 | async-start | bytes 11141120 | tf_op jit(solution)/shard_map/reduce_scatter | solution.py:182
  1012.3 19.1 %all-to-all-start.5 = ((bf16[16,20,1024]{2,1,0:T(8,128)(2,1)}), bf16[16,20,1024]{2,1,0:T(8,128)(2,1)S(1)}, u32[]{:S(2)}, u32[]{:S(2)}) async-start(bf16[16,20,1024]{2,1,0:T(8,128)(2,1)} %copy.125), calls=%async_computation.6 | async-start | bytes 1572864 | tf_op jit(solution)/shard_map/all_to_all | solution.py:190
Sparse Core Ops, SparseCore 0:
  846.5 62.5 all-gather.1
  936.6 73.2 reduce-scatter.1
